TPU v7x, 512 devices: a whole 4x8x8 slice. The times are simulated.
512 devices in a mesh: replica: 32 (over x, y_hi, core), fsdp: 16 (over y_lo, z).
Axes of the slice: x: 4, y: 8 (y_hi: 4, y_lo: 2; y = y_hi * 2 + y_lo), z: 8, core: 2. Of those that a mesh axis runs over, the one named last changes fastest.
Arguments:
- numerators: float32 [32, 4096, 512], P('replica', 'fsdp'), may hold values from -6 to 6
- push_weights: float32 [32], P('replica'), may hold values from 0.5 to 2
- step_power: int32 [1], replicated, may hold values from 0 to 2
- activations: bfloat16 [32, 6144, 4096], P('replica', 'fsdp'), may hold values from -6 to 6
- targets: bfloat16 [32, 6144, 512], P('replica', 'fsdp'), may hold values from -6 to 6
- gain: float32 [4096], replicated, may hold values from 0.1 to 1.9
Outputs:
- mixed_numerators: float32 [32, 4096, 512], P('replica', 'fsdp')
- mixed_weights: float32 [32], P('replica')
All inputs are finite; a program needn't handle non-finite values.
Results may differ from a plain program's by a relative error of at most 0.015.
Values may be sent and summed in bfloat16 or wider, within the bound.
No kernel may reach another device: no remote copies, remote signals or barrier semaphores. Data moves between devices by JAX's collectives and lax.ppermute only.
A program may use at most 64 MiB of HBM per device.

v0:
```python
from functools import partial
import math
import jax
import jax.numpy as jnp
from jax import lax
from jax.sharding import PartitionSpec as P

DIST_KINDS = 3


def passed_along(value, axis, steps):
    count = lax.axis_size(axis)
    pairs = [(source, (source + steps) % count) for source in range(count)]
    return lax.ppermute(value, axis, pairs)


def send_updated(pair, by):
    return passed_along(pair, "replica", by)


def to_peer(sender, operand, power):
    branches = [partial(sender, by=1 << bit) for bit in range(DIST_KINDS)]
    return lax.switch(power, branches, operand)


def body(numerators, push_weights, step_power, activations, targets, gain):
    numer = numerators[0]
    power = step_power[0]
    features = activations.shape[2]
    replica_tokens = activations.shape[1] * lax.axis_size("fsdp")
    params = (numer / push_weights[0]).astype(jnp.bfloat16)
    act32 = activations[0].astype(jnp.float32)
    mean_sq = jnp.mean(act32 * act32, axis=1, keepdims=True)
    normed = (act32 * lax.rsqrt(mean_sq + 1e-05) * gain[None, :]).astype(jnp.bfloat16)
    columns = normed
    keys = jnp.dot(
        columns,
        lax.all_gather(params, "fsdp", axis=0, tiled=True),
        preferred_element_type=jnp.float32,
    ) / math.sqrt(features)
    errors = ((keys - targets[0].astype(jnp.float32)) / math.sqrt(replica_tokens)).astype(
        jnp.bfloat16
    )
    columns = normed
    grad = lax.psum_scatter(
        lax.dot_general(
            columns, errors, (((0,), (0,)), ((), ())), preferred_element_type=jnp.float32
        ).astype(jnp.bfloat16),
        "fsdp",
        scatter_dimension=0,
        tiled=True,
    ).astype(jnp.float32)
    updated = numer - 0.3 * grad
    peer_updated, peer_weight = to_peer(send_updated, (updated, push_weights), power)
    mixed_numerators = 0.5 * (updated + peer_updated)
    mixed_weights = 0.5 * (push_weights + peer_weight)
    return (mixed_numerators[None], mixed_weights)


def solution(mesh):
    return jax.shard_map(
        body,
        mesh=mesh,
        in_specs=(
            P("replica", "fsdp", None),
            P("replica"),
            P(),
            P("replica", "fsdp", None),
            P("replica", "fsdp", None),
            P(),
        ),
        out_specs=(P("replica", "fsdp", None), P("replica")),
        check_vma=False,
    )
```

profile of v0, /device:TPU:8, one launch (start us, length us, event | category | flops | bytes accessed | tf_op | source)
XLA Modules:
  0.0 219.8 jit_solution(8398441809625169285)
XLA Ops:
  7.2 0.0 copy-start
  7.2 0.0 copy-start.2
  7.2 0.0 all-gather.2.cloned.1.call-start
  8.0 2.0 fusion.8
  10.0 0.0 all-gather.2.cloned.1.call-update
  10.1 0.0 reduce-scatter.2.cloned.1.call-start
  10.1 2.6 %fusion = f32[384]{0:T(512)S(1)} fusion(bf16[1,384,4096]{2,1,0:T(8,128)(2,1)} %param.12), kind=kLoop, calls=%fused_computation.2 | loop fusion | flops 4718208 | bytes 3147264 | tf_op jit(solution)/shard_map/reduce_sum | solution.py:33
  12.7 80.8 %all-gather.2.cloned.1.call-done = bf16[4096,512]{1,0:T(8,128)(2,1)} async-done(((bf16[256,512]{1,0:T(8,128)(2,1)}), bf16[4096,512]{1,0:T(8,128)(2,1)}) %all-gather.2.cloned.1.call-update) | async-done | bytes 4194320 | tf_op jit(solution)/shard_map/all_gather | solution.py:38
  93.5 0.0 copy-done
  93.5 0.0 copy-done.2
  93.5 8.4 %convolution_convert_fusion = bf16[4096,512]{1,0:T(8,128)(2,1)} fusion(bf16[1,384,4096]{2,1,0:T(8,128)(2,1)S(1)} %copy-done, f32[4096]{0:T(1024)} %param.14, f32[384]{0:T(512)S(1)} %add_rsqrt_fusion, bf16[4096,512]{1,0:T(8,128)(2,1)} %all-gather.2.cloned.1.call-done, bf16[1,384,512]{2,1,0:T(8,128)(2,1)S(1)} %copy-done.2), kind=kOutput, calls=%fused_computation.5 | convolution fusion | flops 3236888576 | bytes 11945472 | tf_op jit(solution)/shard_map/dot_general | solution.py:46
  101.9 0.0 copy-start.1
  101.9 0.0 reduce-scatter.2.cloned.1.call-update
  102.6 81.1 %reduce-scatter.2.cloned.1.call-done = bf16[256,512]{1,0:T(8,128)(2,1)} async-done(((bf16[4096,512]{1,0:T(8,128)(2,1)}), bf16[256,512]{1,0:T(8,128)(2,1)}) %reduce-scatter.2.cloned.1.call-update) | async-done | bytes 262160 | tf_op jit(solution)/shard_map/reduce_scatter | solution.py:45
  183.7 0.0 copy-done.1
  183.7 1.0 bitcast_subtract_fusion
  184.8 24.5 %conditional.1 = (f32[256,512]{1,0:T(8,128)}, f32[1]{0:T(128)}) conditional(s32[]{:T(128)} %bitcast.5, (f32[256,512]{1,0:T(8,128)S(1)}, f32[1]{0:T(128)}) %tuple.20, (f32[256,512]{1,0:T(8,128)S(1)}, f32[1]{0:T(128)}) %tuple.20, (f32[256,512]{1,0:T(8,128)S(1)}, f32[1]{0:T(128)}) %tuple.20), branch_computations={%region_2.0_spmd, %region_3.0_spmd, %region_4.0_spmd} | conditional | bytes 2097264 | solution.py:23
  184.8 8.9 %collective-permute-start.4 = (f32[256,512]{1,0:T(8,128)S(1)}, f32[256,512]{1,0:T(8,128)}, u32[]{:S(2)}, u32[]{:S(2)}) collective-permute-start(f32[256,512]{1,0:T(8,128)S(1)} %get-tuple-element.16), channel_id=1, source_target_pairs={{0,64},{16,80},{32,96},{48,112},{64,128},{80,144},{96,160},{112,17... | collective-permute-start | bytes 1572872 | tf_op jit(solution)/shard_map/cond/branch_2_fun/ppermute | solution.py:14
  193.7 1.9 collective-permute-start.5
  195.6 13.6 %collective-permute-done.5 = f32[1]{0:T(128)} collective-permute-done((f32[1]{0:T(128)}, f32[1]{0:T(128)}, u32[]{:S(2)}, u32[]{:S(2)}) %collective-permute-start.5) | collective-permute-done | bytes 36 | tf_op jit(solution)/shard_map/cond/branch_2_fun/ppermute | solution.py:14
  209.2 0.0 collective-permute-done.4
  209.2 1.9 multiply_bitcast_fusion
  (1 shorter events, 0.0 us)
Async XLA Ops:
  7.2 86.4 %copy-start = (bf16[1,384,4096]{2,1,0:T(8,128)(2,1)S(1)}, bf16[1,384,4096]{2,1,0:T(8,128)(2,1)}, u32[]{:S(2)}) copy-start(bf16[1,384,4096]{2,1,0:T(8,128)(2,1)} %param.12) | copy-start | bytes 9437188
  7.2 86.3 %copy-start.2 = (bf16[1,384,512]{2,1,0:T(8,128)(2,1)S(1)}, bf16[1,384,512]{2,1,0:T(8,128)(2,1)}, u32[]{:S(2)}) copy-start(bf16[1,384,512]{2,1,0:T(8,128)(2,1)} %param.13) | copy-start | bytes 1179652
  7.2 86.3 %all-gather.2.cloned.1.call-start = ((), (), s32[]{:S(2)}) async-start(), calls=%async_computation.1 | async-start | bytes 4456448 | tf_op jit(solution)/shard_map/all_gather | solution.py:38
  10.1 173.7 %reduce-scatter.2.cloned.1.call-start = ((), (), s32[]{:S(2)}) async-start(), calls=%async_computation.2 | async-start | bytes 4456448 | tf_op jit(solution)/shard_map/reduce_scatter | solution.py:45
  101.9 81.9 %copy-start.1 = (f32[1,256,512]{2,1,0:T(8,128)S(1)}, f32[1,256,512]{2,1,0:T(8,128)}, u32[]{:S(2)}) copy-start(f32[1,256,512]{2,1,0:T(8,128)} %param.9) | copy-start | bytes 1572868
  184.8 24.4 %collective-permute-start.4 = (f32[256,512]{1,0:T(8,128)S(1)}, f32[256,512]{1,0:T(8,128)}, u32[]{:S(2)}, u32[]{:S(2)}) collective-permute-start(f32[256,512]{1,0:T(8,128)S(1)} %get-tuple-element.16), channel_id=1, source_target_pairs={{0,64},{16,80},{32,96},{48,112},{64,128},{80,144},{96,160},{112,17... | collective-permute-start | bytes 1572872 | tf_op jit(solution)/shard_map/cond/branch_2_fun/ppermute | solution.py:14
  193.7 15.5 %collective-permute-start.5 = (f32[1]{0:T(128)}, f32[1]{0:T(128)}, u32[]{:S(2)}, u32[]{:S(2)}) collective-permute-start(f32[1]{0:T(128)} %get-tuple-element.17), channel_id=1, source_target_pairs={{0,64},{16,80},{32,96},{48,112},{64,128},{80,144},{96,160},{112,17... | collective-permute-start | bytes 20 | tf_op jit(solution)/shard_map/cond/branch_2_fun/ppermute | solution.py:14
Sparse Core Ops, SparseCore 0:
  10.6 82.8 all-gather.1
  102.0 81.6 reduce-scatter.1
where the time goes:
time: 220 us
  waiting for transfers between devices  176 us (80%)
  between operations  17.3 us (8%)
  starting transfers between devices  10.9 us (5%)
  matrix products  8.36 us (4%)
  other arithmetic  7.54 us (3%)
    reduce_scatter x1, waiting for transfers between devices, body(): lax.psum_scatter(lax.dot_general(columns, errors, (((0,), (0,)), ((), ())...  81.1 us
    all_gather x1, waiting for transfers between devices, body(): lax.all_gather(params, 'fsdp', axis=0, tiled=True)  80.8 us
    ppermute x2, waiting for transfers between devices, passed_along(): return lax.ppermute(value, axis, pairs)  13.6 us
    ppermute x2, starting transfers between devices, passed_along(): return lax.ppermute(value, axis, pairs)  10.8 us
    dot_general x1, matrix products, body(): lax.dot_general(columns, errors, (((0,), (0,)), ((), ())), preferred_elem...  8.36 us
  transfers between devices with their start and end apart: 4, of which 3 were waited for; matrix products, arithmetic and copies ran while one was open for 1% of the time, Pallas kernels for 0%

commit v1 on v0

--- a/solution.py
+++ b/solution.py
@@ -35,7 +35,9 @@
     columns = normed
     keys = jnp.dot(
         columns,
-        lax.all_gather(params, "fsdp", axis=0, tiled=True),
+        jnp.concatenate(
+            lax.all_to_all(jnp.stack([params] * lax.axis_size("fsdp")), "fsdp", 0, 0), axis=0
+        ),
         preferred_element_type=jnp.float32,
     ) / math.sqrt(features)
     errors = ((keys - targets[0].astype(jnp.float32)) / math.sqrt(replica_tokens)).astype(

time: 220 us -> 258 us (1.17)
  the two profiles are of different devices: /device:TPU:8 before, /device:TPU:24 now
where the time goes in v1:
time: 258 us; the launch traced here: 257 us
  waiting for transfers between devices  201 us (78%)
  starting transfers between devices  24 us (9%)
  between operations  17.1 us (7%)
  matrix products  8.38 us (3%)
  other arithmetic  4.73 us (2%)
    all_to_all x1, waiting for transfers between devices, body(): lax.all_to_all(jnp.stack([params] * lax.axis_size('fsdp')), 'fsdp', 0, 0)  105 us
    reduce_scatter x1, waiting for transfers between devices, body(): lax.psum_scatter(lax.dot_general(columns, errors, (((0,), (0,)), ((), ())...  82.4 us
    ppermute x2, waiting for transfers between devices, passed_along(): return lax.ppermute(value, axis, pairs)  12.8 us
    all_to_all x1, starting transfers between devices, body(): lax.all_to_all(jnp.stack([params] * lax.axis_size('fsdp')), 'fsdp', 0, 0)  12.1 us
    ppermute x2, starting transfers between devices, passed_along(): return lax.ppermute(value, axis, pairs)  12 us
    dot_general x1, matrix products, body(): lax.dot_general(columns, errors, (((0,), (0,)), ((), ())), preferred_elem...  8.38 us
  transfers between devices with their start and end apart: 4, of which 3 were waited for; matrix products, arithmetic and copies ran while one was open for 0% of the time, Pallas kernels for 0%

profile of v1, /device:TPU:24, one launch (start us, length us, event | category | flops | bytes accessed | tf_op | source)
XLA Modules:
  0.0 257.3 jit_solution(362780594197579538)
XLA Ops:
  7.8 1.1 fusion.27
  8.9 2.4 stack.5
  11.3 0.0 copy-start
  11.3 0.0 copy-start.2
  11.3 12.1 %all-to-all-start = ((bf16[16,256,512]{2,1,0:T(8,128)(2,1)}), bf16[16,256,512]{2,1,0:T(8,128)(2,1)}, u32[]{:S(2)}, u32[]{:S(2)}) async-start(bf16[16,256,512]{2,1,0:T(8,128)(2,1)} %stack.5), calls=%async_computation | async-start | bytes 8388608 | tf_op jit(solution)/shard_map/all_to_all | solution.py:39
  23.3 0.0 reduce-scatter.2.cloned.1.call-start
  23.4 0.0 copy-done
  23.4 0.7 fusion.2
  24.1 105.3 %all-to-all-done = bf16[16,256,512]{2,1,0:T(8,128)(2,1)} async-done(((bf16[16,256,512]{2,1,0:T(8,128)(2,1)}), bf16[16,256,512]{2,1,0:T(8,128)(2,1)}, u32[]{:S(2)}, u32[]{:S(2)}) %all-to-all-start) | async-done | bytes 4194336 | tf_op jit(solution)/shard_map/all_to_all | solution.py:39
  129.4 0.0 copy-done.2
  129.4 8.4 %convolution_convert_fusion = bf16[4096,512]{1,0:T(8,128)(2,1)} fusion(bf16[1,384,4096]{2,1,0:T(8,128)(2,1)S(1)} %copy-done, f32[4096]{0:T(1024)} %param.14, f32[384]{0:T(512)S(1)} %add_rsqrt_fusion, bf16[4096,512]{1,0:T(8,128)(2,1)} %bitcast.5, bf16[1,384,512]{2,1,0:T(8,128)(2,1)S(1)} %copy-done.2), kind=kOutput, calls=%fused_computation.9 | convolution fusion | flops 3236888576 | bytes 11945472 | tf_op jit(solution)/shard_map/dot_general | solution.py:48
  137.8 0.0 copy-start.1
  137.8 0.0 reduce-scatter.2.cloned.1.call-update
  138.5 82.4 %reduce-scatter.2.cloned.1.call-done = bf16[256,512]{1,0:T(8,128)(2,1)} async-done(((bf16[4096,512]{1,0:T(8,128)(2,1)}), bf16[256,512]{1,0:T(8,128)(2,1)}) %reduce-scatter.2.cloned.1.call-update) | async-done | bytes 262160 | tf_op jit(solution)/shard_map/reduce_scatter | solution.py:47
  220.9 0.0 copy-done.1
  220.9 1.0 bitcast_subtract_fusion
  222.0 24.8 %conditional.1 = (f32[256,512]{1,0:T(8,128)}, f32[1]{0:T(128)}) conditional(s32[]{:T(128)} %bitcast.7, (f32[256,512]{1,0:T(8,128)S(1)}, f32[1]{0:T(128)}) %tuple.20, (f32[256,512]{1,0:T(8,128)S(1)}, f32[1]{0:T(128)}) %tuple.20, (f32[256,512]{1,0:T(8,128)S(1)}, f32[1]{0:T(128)}) %tuple.20), branch_computations={%region_2.0_spmd, %region_3.0_spmd, %region_4.0_spmd} | conditional | bytes 2097264 | solution.py:23
  222.0 10.0 %collective-permute-start.4 = (f32[256,512]{1,0:T(8,128)S(1)}, f32[256,512]{1,0:T(8,128)}, u32[]{:S(2)}, u32[]{:S(2)}) collective-permute-start(f32[256,512]{1,0:T(8,128)S(1)} %get-tuple-element.16), channel_id=1, source_target_pairs={{0,64},{16,80},{32,96},{48,112},{64,128},{80,144},{96,160},{112,17... | collective-permute-start | bytes 1572872 | tf_op jit(solution)/shard_map/cond/branch_2_fun/ppermute | solution.py:14
  232.0 1.9 collective-permute-start.5
  233.9 12.8 %collective-permute-done.5 = f32[1]{0:T(128)} collective-permute-done((f32[1]{0:T(128)}, f32[1]{0:T(128)}, u32[]{:S(2)}, u32[]{:S(2)}) %collective-permute-start.5) | collective-permute-done | bytes 36 | tf_op jit(solution)/shard_map/cond/branch_2_fun/ppermute | solution.py:14
  246.8 0.0 collective-permute-done.4
  246.8 1.9 multiply_bitcast_fusion
  (1 shorter events, 0.0 us)
Async XLA Ops:
  11.3 12.1 %copy-start = (bf16[1,384,4096]{2,1,0:T(8,128)(2,1)S(1)}, bf16[1,384,4096]{2,1,0:T(8,128)(2,1)}, u32[]{:S(2)}) copy-start(bf16[1,384,4096]{2,1,0:T(8,128)(2,1)} %param.12) | copy-start | bytes 9437188
  11.3 118.1 %copy-start.2 = (bf16[1,384,512]{2,1,0:T(8,128)(2,1)S(1)}, bf16[1,384,512]{2,1,0:T(8,128)(2,1)}, u32[]{:S(2)}) copy-start(bf16[1,384,512]{2,1,0:T(8,128)(2,1)} %param.13) | copy-start | bytes 1179652
  11.3 118.1 %all-to-all-start = ((bf16[16,256,512]{2,1,0:T(8,128)(2,1)}), bf16[16,256,512]{2,1,0:T(8,128)(2,1)}, u32[]{:S(2)}, u32[]{:S(2)}) async-start(bf16[16,256,512]{2,1,0:T(8,128)(2,1)} %stack.5), calls=%async_computation | async-start | bytes 8388608 | tf_op jit(solution)/shard_map/all_to_all | solution.py:39
  23.3 197.6 %reduce-scatter.2.cloned.1.call-start = ((), (), s32[]{:S(2)}) async-start(), calls=%async_computation.2 | async-start | bytes 4456448 | tf_op jit(solution)/shard_map/reduce_scatter | solution.py:47
  137.8 83.1 %copy-start.1 = (f32[1,256,512]{2,1,0:T(8,128)S(1)}, f32[1,256,512]{2,1,0:T(8,128)}, u32[]{:S(2)}) copy-start(f32[1,256,512]{2,1,0:T(8,128)} %param.9) | copy-start | bytes 1572868
  222.0 24.8 %collective-permute-start.4 = (f32[256,512]{1,0:T(8,128)S(1)}, f32[256,512]{1,0:T(8,128)}, u32[]{:S(2)}, u32[]{:S(2)}) collective-permute-start(f32[256,512]{1,0:T(8,128)S(1)} %get-tuple-element.16), channel_id=1, source_target_pairs={{0,64},{16,80},{32,96},{48,112},{64,128},{80,144},{96,160},{112,17... | collective-permute-start | bytes 1572872 | tf_op jit(solution)/shard_map/cond/branch_2_fun/ppermute | solution.py:14
  232.0 14.8 %collective-permute-start.5 = (f32[1]{0:T(128)}, f32[1]{0:T(128)}, u32[]{:S(2)}, u32[]{:S(2)}) collective-permute-start(f32[1]{0:T(128)} %get-tuple-element.17), channel_id=1, source_target_pairs={{0,64},{16,80},{32,96},{48,112},{64,128},{80,144},{96,160},{112,17... | collective-permute-start | bytes 20 | tf_op jit(solution)/shard_map/cond/branch_2_fun/ppermute | solution.py:14
Sparse Core Ops, SparseCore 0:
  137.9 82.9 reduce-scatter.1
